TPU v7x, 128 devices: a whole 4x4x4 slice. The times are simulated.
128 devices in a mesh: req: 4 (over y), head: 32 (over x, z, core).
Axes of the slice: x: 4, y: 4, z: 4, core: 2. Of those that a mesh axis runs over, the one named last changes fastest.
Arguments:
- hidden_in: bfloat16 [8192, 2048], P(('req', 'head')), may hold values from -6 to 6
- queries: bfloat16 [8192, 2048], P(('req', 'head')), may hold values from -160 to 160
- keys_values: bfloat16 [8192, 1024], P(('req', 'head')), may hold values from -10 to 10
- request_of_row: int32 [8192], P('req'), may hold values from 0 to 7, as said below
- page_route: int32 [4, 32, 4], P('req', 'head'), may hold values from 0 to 3, each once within a row
- expert_ids: int32 [8192, 6], P(('req', 'head')), may hold values from 0 to 31, all different within a row; in each aligned block of 64 rows (0 to 63, 64 to 127, ...) at most 14 rows name the same one
- expert_weights: float32 [8192, 6], P(('req', 'head')), may hold values from 0.05 to 0.5
- norm_gain: float32 [2048], replicated, may hold values from 0.25 to 1.75
- shared_gate_up: bfloat16 [2048, 2, 1408], replicated, may hold values from -0.125 to 0.125
- shared_down: bfloat16 [1408, 2048], replicated, may hold values from -0.15625 to 0.15625
- expert_gate_up: bfloat16 [32, 2, 1408, 2048], P('head', None, 'req'), may hold values from -0.125 to 0.125
- expert_down: bfloat16 [32, 1408, 2048], P('head', 'req'), may hold values from -0.15625 to 0.15625
Outputs:
- layer_out: bfloat16 [8192, 2048], P(('req', 'head'))
Inputs may be any that keep to these rules, and one draw needn't show every extreme that they name: `request_of_row`: each group of 2048 rows g holds two requests, ids 2 g then 2 g + 1, each a whole number of pages of 16 rows and at least 128 rows long. `page_route`: for every device, the groups receiving its pages form a permutation of all groups. `expert_ids`: each row names 6 different experts; among the rows of one device no expert is named more than 14 times, and some device names some expert exactly 14 times.
All inputs are finite; a program needn't handle non-finite values.
Results may differ from a plain program's by a relative error of at most 0.006.
Values may be sent and summed in bfloat16 or wider, within the bound.
No kernel may reach another device: no remote copies, remote signals or barrier semaphores. Data moves between devices by JAX's collectives and lax.ppermute only.
A program may use at most 192 MiB of HBM per device.

v0:
```python
import jax
import jax.numpy as jnp
from jax import lax
from jax.sharding import PartitionSpec as P

QUERY_HEADS = 16
KEY_VALUE_HEADS = 4
HEAD_SIZE = 128
EXPERTS = 32
TOP = 6
CAP = 14
negative_large = -1e30


def silu_mul(gate_value, upward):
    return gate_value / (1.0 + jnp.exp(-gate_value)) * upward


def body(
    hidden_in,
    queries,
    keys_values,
    request_of_row,
    page_route,
    expert_ids,
    expert_weights,
    norm_gain,
    shared_gate_up,
    shared_down,
    expert_gate_up,
    expert_down,
):
    groups = lax.axis_size("req")
    columns = lax.axis_size("head")
    token_rows = hidden_in.shape[0]
    model_width = hidden_in.shape[1]
    page_rows = token_rows // groups
    group_ids = jnp.arange(groups, dtype=jnp.int32)
    page_dest = page_route.reshape(groups)
    matches = (page_dest[None, :] == group_ids[:, None]).astype(jnp.int32)
    dest_order = jnp.sum(matches * group_ids[None, :], axis=1)

    def by_dest(array_in):
        return jnp.take(array_in.reshape(groups, page_rows, array_in.shape[1]), dest_order, axis=0)

    widths = (hidden_in.shape[1], queries.shape[1], keys_values.shape[1])
    packed = jnp.concatenate((hidden_in, queries, keys_values), axis=1)
    moved = lax.all_to_all(by_dest(packed), "req", split_axis=0, concat_axis=0, tiled=True)
    moved = moved.reshape(token_rows, sum(widths))
    resid = moved[:, : widths[0]]
    rows_of_queries = moved[:, widths[0] : widths[0] + widths[1]]
    key_value_rows = moved[:, widths[0] + widths[1] :]
    group_fraction = QUERY_HEADS // KEY_VALUE_HEADS
    key_value_width = KEY_VALUE_HEADS * HEAD_SIZE
    score_scale = HEAD_SIZE ** (-0.5)
    query_start = lax.axis_index("head") * token_rows
    segment_query = lax.dynamic_slice_in_dim(request_of_row, query_start, token_rows)
    position_query = query_start + jnp.arange(token_rows, dtype=jnp.int32)
    query_fourfold = rows_of_queries.reshape(token_rows, KEY_VALUE_HEADS, group_fraction, HEAD_SIZE)
    start_state = (
        jnp.full((KEY_VALUE_HEADS, group_fraction, token_rows), negative_large, jnp.float32),
        jnp.zeros((KEY_VALUE_HEADS, group_fraction, token_rows), jnp.float32),
        jnp.zeros((KEY_VALUE_HEADS, group_fraction, token_rows, HEAD_SIZE), jnp.float32),
    )
    kv_piece = lax.all_gather(key_value_rows, "head", axis=0, tiled=True)
    piece_rows = kv_piece.shape[0]
    rows_per_block = 512

    def one_block(block_index, carried_block):
        offset = block_index * rows_per_block
        current_block = lax.dynamic_slice_in_dim(kv_piece, offset, rows_per_block)
        block_keys = current_block[:, :key_value_width].reshape(
            rows_per_block, KEY_VALUE_HEADS, HEAD_SIZE
        )
        block_values = current_block[:, key_value_width:].reshape(
            rows_per_block, KEY_VALUE_HEADS, HEAD_SIZE
        )
        segment_key = lax.dynamic_slice_in_dim(request_of_row, offset, rows_per_block)
        position_key = offset + jnp.arange(rows_per_block, dtype=jnp.int32)
        allowed = (segment_query[:, None] == segment_key[None, :]) & (
            position_key[None, :] <= position_query[:, None]
        )
        running_max, running_sum, accumulated = carried_block
        score = (
            jnp.einsum(
                "tgqd,sgd->gqts", query_fourfold, block_keys, preferred_element_type=jnp.float32
            )
            * score_scale
        )
        masked = jnp.where(allowed, score, negative_large)
        new_max = jnp.maximum(running_max, jnp.max(masked, axis=-1))
        weights = jnp.where(allowed, jnp.exp(masked - new_max[..., None]), 0.0)
        factor = jnp.exp(running_max - new_max)
        running_sum = running_sum * factor + jnp.sum(weights, axis=-1)
        accumulated = accumulated * factor[..., None] + jnp.einsum(
            "gqts,sgd->gqtd",
            weights.astype(jnp.bfloat16),
            block_values,
            preferred_element_type=jnp.float32,
        )
        return (new_max, running_sum, accumulated)

    running_max, running_sum, accumulated = lax.fori_loop(
        0, piece_rows // rows_per_block, one_block, start_state
    )
    context = jnp.transpose(accumulated / running_sum[..., None], (2, 0, 1, 3)).reshape(
        token_rows, QUERY_HEADS * HEAD_SIZE
    )
    mixed_rows = resid.astype(jnp.float32) + context
    mean_square = jnp.mean(mixed_rows * mixed_rows, axis=1, keepdims=True)
    normed = (mixed_rows * lax.rsqrt(mean_square + 1e-06) * norm_gain).astype(jnp.bfloat16)
    pair_expert = expert_ids.reshape(-1)
    hit_table = (pair_expert[:, None] == jnp.arange(EXPERTS, dtype=jnp.int32)[None, :]).astype(
        jnp.int32
    )
    ranks = jnp.sum((jnp.cumsum(hit_table, axis=0) - 1) * hit_table, axis=1)
    slot_of = pair_expert * CAP + ranks
    slots_all = EXPERTS * CAP
    placing = jnp.arange(slots_all, dtype=jnp.int32)[:, None] == slot_of[None, :]
    placing = jnp.any(placing.reshape(slots_all, token_rows, TOP), axis=2).astype(jnp.bfloat16)
    outgoing = jnp.dot(placing, normed, preferred_element_type=jnp.float32).astype(jnp.bfloat16)
    local_experts = expert_gate_up.shape[0]
    outgoing = outgoing.reshape(columns, local_experts * CAP, model_width)
    shared_both = jnp.dot(
        normed, shared_gate_up.reshape(model_width, -1), preferred_element_type=jnp.float32
    ).reshape(token_rows, 2, -1)
    shared_hidden = silu_mul(shared_both[:, 0], shared_both[:, 1]).astype(jnp.bfloat16)
    shared_out = jnp.dot(shared_hidden, shared_down, preferred_element_type=jnp.float32)
    at_expert = lax.all_to_all(outgoing, "head", split_axis=0, concat_axis=0, tiled=True)
    gathered = lax.all_gather(at_expert, "req", axis=0, tiled=True)
    expert_rows = gathered.reshape(-1, model_width)
    both_parts = jnp.einsum(
        "nd,kfd->nkf", expert_rows, expert_gate_up[0], preferred_element_type=jnp.float32
    )
    hidden = silu_mul(both_parts[:, 0], both_parts[:, 1]).astype(jnp.bfloat16)
    part_out = jnp.dot(hidden, expert_down[0], preferred_element_type=jnp.float32).astype(
        jnp.bfloat16
    )
    part_sum = lax.psum_scatter(part_out, "req", scatter_dimension=0, tiled=True)
    returned = lax.all_to_all(
        part_sum.reshape(columns, local_experts * CAP, model_width),
        "head",
        split_axis=0,
        concat_axis=0,
        tiled=True,
    )
    summed = returned.reshape(slots_all, model_width)
    pair_rows = jnp.take(summed, slot_of, axis=0).reshape(token_rows, TOP, model_width)
    routed = jnp.sum(pair_rows.astype(jnp.float32) * expert_weights[:, :, None], axis=1)
    return (mixed_rows + shared_out + routed).astype(jnp.bfloat16)


def solution(mesh):
    return jax.shard_map(
        body,
        mesh=mesh,
        in_specs=(
            P(("req", "head"), None),
            P(("req", "head"), None),
            P(("req", "head"), None),
            P("req"),
            P("req", "head", None),
            P(("req", "head"), None),
            P(("req", "head"), None),
            P(),
            P(),
            P(),
            P("head", None, "req", None),
            P("head", "req", None),
        ),
        out_specs=P(("req", "head"), None),
        check_vma=False,
    )
```

profile of v0, /device:TPU:1, one launch (start us, length us, event | category | flops | bytes accessed | tf_op | source)
XLA Modules:
  0.0 419.0 jit_solution(10034668112566596704)
XLA Ops:
  11.3 14.8 %all_to_all.15 = bf16[4,16,5120]{2,1,0:T(8,128)(2,1)S(1)} all-to-all(bf16[4,16,5120]{2,1,0:T(8,128)(2,1)S(1)} %broadcast_select_fusion), channel_id=1, replica_groups=mesh['req'=4,'head'=32] {'req'}, dimensions={0} | all-to-all | bytes 1310720 | tf_op jit(solution)/shard_map/all_to_all | solution.py:48
  32.5 2.6 reduce-window.6
  49.9 25.2 %all-gather.3.cloned.1.call-done = bf16[2048,1024]{1,0:T(8,128)(2,1)} async-done(((bf16[64,1024]{1,0:T(8,128)(2,1)}), bf16[2048,1024]{1,0:T(8,128)(2,1)}) %all-gather.3.cloned.1.call-update) | async-done | bytes 4194320 | tf_op jit(solution)/shard_map/all_gather | solution.py:65
  75.0 43.0 %while.18 = (s32[]{:T(128)}, f32[4,4,64]{2,1,0:T(4,128)S(1)}, f32[4,4,64]{2,1,0:T(4,128)S(1)}, f32[4,4,64,128]{3,2,1,0:T(8,128)}, s32[64]{0:T(128)}, /*index=5*/...) while((s32[]{:T(128)}, f32[4,4,64]{2,1,0:T(4,128)S(1)}, ...), condition=%wide.region_4.5_spmd.clone, body=%wide.region_1.4_spmd.clone.sunk | while | flops 275748416 | bytes 19344444 | solution.py:103
  87.3 2.1 fusion.59
  126.5 3.6 reshape.171
  130.2 33.4 %all_to_all.16 = bf16[32,14,2048]{2,1,0:T(8,128)(2,1)S(1)} all-to-all(bf16[32,14,2048]{2,1,0:T(8,128)(2,1)} %reshape.171), channel_id=1, replica_groups=mesh['req'=4,'head'=32] {'head'}, dimensions={0} | all-to-all | bytes 3670016 | tf_op jit(solution)/shard_map/all_to_all | solution.py:129
  163.6 2.3 copy.68
  166.1 71.6 %all-gather.5.cloned.1.call-done = bf16[128,14,2048]{2,0,1:T(8,128)(2,1)} async-done(((bf16[32,14,2048]{2,0,1:T(8,128)(2,1)}), bf16[128,14,2048]{2,0,1:T(8,128)(2,1)}) %all-gather.5.cloned.1.call-update) | async-done | bytes 7340048 | tf_op jit(solution)/shard_map/all_gather | solution.py:130
  237.8 10.4 %copy.69 = bf16[128,14,2048]{2,1,0:T(8,128)(2,1)} copy(bf16[128,14,2048]{2,0,1:T(8,128)(2,1)} %all-gather.5.cloned.1.call-done) | data formatting | bytes 14680064 | tf_op jit(solution)/shard_map/all_gather | solution.py:130
  248.2 10.5 %reshape.196 = bf16[1792,2048,1]{1,0,2:T(8,128)(2,1)} reshape(bf16[128,14,2048]{2,1,0:T(8,128)(2,1)} %copy.69) | data formatting | bytes 14680064 | tf_op jit(solution)/shard_map/reshape | solution.py:131
  258.7 8.6 %fusion.14 = f32[1792,2,352]{0,2,1:T(8,128)S(1)} fusion(bf16[1792,2048,1]{1,0,2:T(8,128)(2,1)} %reshape.196, bf16[1,2,352,2048]{3,2,1,0:T(8,128)(2,1)S(1)} %copy-done), kind=kOutput, calls=%fused_computation.28 | convolution fusion | flops 5167382528 | bytes 15269888 | tf_op jit(solution)/shard_map/nd,kfd->nkf/dot_general | solution.py:132
  267.3 6.2 %convolution_convert_fusion = bf16[1792,2048]{1,0:T(8,128)(2,1)} fusion(bf16[1,352,2048]{2,1,0:T(8,128)(2,1)S(1)} %copy-done.15, f32[1792,2,352]{0,2,1:T(8,128)S(1)} %fusion.14), kind=kOutput, calls=%fused_computation.25 | convolution fusion | flops 2590515200 | bytes 13828096 | tf_op jit(solution)/shard_map/dot_general | solution.py:136
  273.5 73.6 %reduce-scatter.2.cloned.1.call-done = bf16[448,2048]{1,0:T(8,128)(2,1)} async-done(((bf16[1792,2048]{1,0:T(8,128)(2,1)}), bf16[448,2048]{1,0:T(8,128)(2,1)}) %reduce-scatter.2.cloned.1.call-update) | async-done | bytes 1835024 | tf_op jit(solution)/shard_map/reduce_scatter | solution.py:139
  347.1 3.6 reshape.173
  350.7 7.9 %all-to-all-start.2 = ((bf16[32,14,2048]{2,1,0:T(8,128)(2,1)}), bf16[32,14,2048]{2,1,0:T(8,128)(2,1)}, u32[]{:S(2)}, u32[]{:S(2)}) async-start(bf16[32,14,2048]{2,1,0:T(8,128)(2,1)} %reshape.173), calls=%async_computation.3 | async-start | bytes 4194304 | tf_op jit(solution)/shard_map/all_to_all | solution.py:140
  359.2 11.3 %copy.82 = bf16[256,8,2,1408]{3,1,2,0:T(8,128)(2,1)} copy(bf16[256,8,2,1408]{3,2,1,0:T(2,128)(2,1)} %bitcast.103) | data formatting | bytes 23068672
  370.4 15.2 %copy.62 = bf16[2816,2048]{1,0:T(8,128)(2,1)} copy(bf16[2816,2048]{0,1:T(8,128)(2,1)} %bitcast.101) | data formatting | bytes 23068672 | tf_op jit(solution)/shard_map/dot_general | solution.py:124
  385.7 8.7 %fusion.25 = f32[64,2,1408]{2,0,1:T(8,128)} fusion(bf16[2,1408,2048]{2,1,0:T(8,128)(2,1)} %bitcast.100, bf16[64,2048]{1,0:T(8,128)(2,1)S(1)} %copy-done.6), kind=kOutput, calls=%fused_computation.49 | convolution fusion | flops 738197504 | bytes 12517376 | tf_op jit(solution)/shard_map/dot_general | solution.py:124
  394.4 2.5 reshape.174
  396.9 3.1 gather_fusion.1
  400.1 3.7 gather.12
  403.8 4.2 multiply_reduce_fusion
  407.9 4.5 %fusion.18 = bf16[64,2048]{1,0:T(8,128)(2,1)} fusion(f32[64,2048]{1,0:T(8,128)S(1)} %multiply_reduce_fusion, bf16[1408,2048]{1,0:T(8,128)(2,1)} %param.23, f32[64,2,1408]{2,0,1:T(8,128)S(1)} %copy-done.4, f32[64,2048]{1,0:T(8,128)S(1)} %reshape.167, bf16[64,5120]{1,0:T(8,128)(2,1)} %bitcast.108), kind=kOutput, calls=%fused_computation.34 | convolution fusion | flops 370204672 | bytes 8060928 | tf_op jit(solution)/shard_map/dot_general | solution.py:128
  (148 shorter events, 75.7 us)
Async XLA Ops:
  6.5 252.2 %copy-start = (bf16[1,2,352,2048]{3,2,1,0:T(8,128)(2,1)S(1)}, bf16[1,2,352,2048]{3,2,1,0:T(8,128)(2,1)}, u32[]{:S(2)}) copy-start(bf16[1,2,352,2048]{3,2,1,0:T(8,128)(2,1)} %param.24) | copy-start | bytes 8650756
  6.5 68.5 %all-gather.3.cloned.1.call-start = ((), (), s32[]{:S(2)}) async-start(), calls=%async_computation.4 | async-start | bytes 4325376 | tf_op jit(solution)/shard_map/all_gather | solution.py:65
  26.1 48.9 %copy-start.3 = (bf16[4,16,5120]{2,1,0:T(8,128)(2,1)}, bf16[4,16,5120]{2,1,0:T(8,128)(2,1)S(1)}, u32[]{:S(2)}) copy-start(bf16[4,16,5120]{2,1,0:T(8,128)(2,1)S(1)} %all_to_all.15) | copy-start | bytes 1966084
  26.8 210.9 %all-gather.5.cloned.1.call-start = ((), (), s32[]{:S(2)}) async-start(), calls=%async_computation.5 | async-start | bytes 9175040 | tf_op jit(solution)/shard_map/all_gather | solution.py:130
  81.7 2.5 copy-start.2
  81.7 2.5 copy-start.7
  92.4 2.5 copy-start.2
  92.4 2.5 copy-start.7
  103.2 2.5 copy-start.2
  103.2 2.5 copy-start.7
  113.9 2.5 copy-start.2
  113.9 2.5 copy-start.7
  118.0 4.8 %copy-start.12 = (f32[2048]{0:T(1024)S(1)}, f32[2048]{0:T(1024)}, u32[]{:S(2)}) copy-start(f32[2048]{0:T(1024)} %param.21) | copy-start | bytes 24580
  119.3 5.3 %copy-start.9 = (pred[448,64]{0,1:T(8,128)(4,1)S(1)}, pred[448,64]{0,1:T(8,128)(4,1)}, u32[]{:S(2)}) copy-start(pred[448,64]{0,1:T(8,128)(4,1)} %fusion.22) | copy-start | bytes 86020
  165.9 181.2 %reduce-scatter.2.cloned.1.call-start = ((), (), s32[]{:S(2)}) async-start(), calls=%async_computation.6 | async-start | bytes 9175040 | tf_op jit(solution)/shard_map/reduce_scatter | solution.py:139
  258.7 8.6 %copy-start.15 = (bf16[1,352,2048]{2,1,0:T(8,128)(2,1)S(1)}, bf16[1,352,2048]{2,1,0:T(8,128)(2,1)}, u32[]{:S(2)}) copy-start(bf16[1,352,2048]{2,1,0:T(8,128)(2,1)} %param.25) | copy-start | bytes 4325380
  350.7 8.0 %copy-start.10 = (s32[64,6]{0,1:T(8,128)S(1)}, s32[64,6]{0,1:T(8,128)}, u32[]{:S(2)}) copy-start(s32[64,6]{0,1:T(8,128)} %param.19) | copy-start | bytes 4612
  350.7 8.2 %copy-start.13 = (f32[64,6]{0,1:T(8,128)S(1)}, f32[64,6]{0,1:T(8,128)}, u32[]{:S(2)}) copy-start(f32[64,6]{0,1:T(8,128)} %param.20) | copy-start | bytes 4612
  350.7 8.3 %copy-start.14 = (pred[64,6]{0,1:T(8,128)(4,1)S(1)}, pred[64,6]{0,1:T(8,128)(4,1)}, u32[]{:S(2)}) copy-start(pred[64,6]{0,1:T(8,128)(4,1)} %get-tuple-element.260) | copy-start | bytes 1156
  350.7 43.7 %all-to-all-start.2 = ((bf16[32,14,2048]{2,1,0:T(8,128)(2,1)}), bf16[32,14,2048]{2,1,0:T(8,128)(2,1)}, u32[]{:S(2)}, u32[]{:S(2)}) async-start(bf16[32,14,2048]{2,1,0:T(8,128)(2,1)} %reshape.173), calls=%async_computation.3 | async-start | bytes 4194304 | tf_op jit(solution)/shard_map/all_to_all | solution.py:140
  370.4 15.2 %copy-start.11 = (s32[384]{0:T(512)S(1)}, s32[384]{0:T(512)}, u32[]{:S(2)}) copy-start(s32[384]{0:T(512)} %fusion.30) | copy-start | bytes 4612
  370.4 15.2 %copy-start.6 = (bf16[64,2048]{1,0:T(8,128)(2,1)S(1)}, bf16[64,2048]{1,0:T(8,128)(2,1)}, u32[]{:S(2)}) copy-start(bf16[64,2048]{1,0:T(8,128)(2,1)} %copy-done.5) | copy-start | bytes 786436
  403.8 4.2 copy-start.4
  403.8 8.7 %copy-start.1 = (bf16[1,2,352,2048]{3,2,1,0:T(8,128)(2,1)S(1)}, bf16[1,2,352,2048]{3,2,1,0:T(8,128)(2,1)}, u32[]{:S(2)}) copy-start(bf16[1,2,352,2048]{3,2,1,0:T(8,128)(2,1)} %param.24) | copy-start | bytes 8650756
  (5 other events, 3.9 us)
Sparse Core Ops, SparseCore 0:
  27.0 48.0 all-gather.2
  166.0 71.7 all-gather.4
  273.6 73.4 reduce-scatter.1
where the time goes:
time: 422 us; the launch traced here: 419 us
  waiting for transfers between devices  170 us (40%)
  local copies, waits for them, and re-layouts  113 us (27%)
  blocking collectives  48.3 us (11%)
  matrix products  40.1 us (10%)
  other arithmetic  25 us (6%)
  between operations  13.3 us (3%)
  starting transfers between devices  8.2 us (2%)
    reduce_scatter x1, waiting for transfers between devices, body(): lax.psum_scatter(part_out, 'req', scatter_dimension=0, tiled=True)  73.6 us
    all_gather x1, waiting for transfers between devices, body(): gathered = lax.all_gather(at_expert, 'req', axis=0, tiled=True)  71.6 us
    all_to_all x1, blocking collectives, body(): lax.all_to_all(outgoing, 'head', split_axis=0, concat_axis=0, tiled=True)  33.4 us
    all_gather x1, waiting for transfers between devices, body(): kv_piece = lax.all_gather(key_value_rows, 'head', axis=0, tiled=True)  25.2 us
    while x36, local copies, waits for them, and re-layouts  15.5 us
    unnamed x30, local copies, waits for them, and re-layouts  15.2 us
    dot_general x1, local copies, waits for them, and re-layouts, body(): jnp.dot(normed, shared_gate_up.reshape(model_width, -1), preferred_elemen...  15.2 us
    all_to_all x1, blocking collectives, body(): lax.all_to_all(by_dest(packed), 'req', split_axis=0, concat_axis=0, tiled...  14.8 us
  transfers between devices with their start and end apart: 4, of which 3 were waited for; matrix products, arithmetic and copies ran while one was open for 14% of the time, Pallas kernels for 0%

commit v1 on v0

--- a/solution.py
+++ b/solution.py
@@ -10,6 +10,24 @@
 TOP = 6
 CAP = 14
 negative_large = -1e30
+
+
+def gather_around(value, axis, dim):
+    ways, here, step = (lax.axis_size(axis), lax.axis_index(axis), value.shape[dim])
+    dims = [n * ways if d == dim else n for d, n in enumerate(value.shape)]
+    full = lax.dynamic_update_slice_in_dim(
+        jnp.zeros(dims, value.dtype), value, here * step, axis=dim
+    )
+    going_up = going_down = value
+    for far in range(1, ways // 2 + 1):
+        going_up = lax.ppermute(going_up, axis, [(d, (d + 1) % ways) for d in range(ways)])
+        full = lax.dynamic_update_slice_in_dim(full, going_up, (here - far) % ways * step, axis=dim)
+        if 2 * far < ways:
+            going_down = lax.ppermute(going_down, axis, [(d, (d - 1) % ways) for d in range(ways)])
+            full = lax.dynamic_update_slice_in_dim(
+                full, going_down, (here + far) % ways * step, axis=dim
+            )
+    return full
 
 
 def silu_mul(gate_value, upward):
@@ -127,7 +145,7 @@
     shared_hidden = silu_mul(shared_both[:, 0], shared_both[:, 1]).astype(jnp.bfloat16)
     shared_out = jnp.dot(shared_hidden, shared_down, preferred_element_type=jnp.float32)
     at_expert = lax.all_to_all(outgoing, "head", split_axis=0, concat_axis=0, tiled=True)
-    gathered = lax.all_gather(at_expert, "req", axis=0, tiled=True)
+    gathered = gather_around(at_expert, "req", 0)
     expert_rows = gathered.reshape(-1, model_width)
     both_parts = jnp.einsum(
         "nd,kfd->nkf", expert_rows, expert_gate_up[0], preferred_element_type=jnp.float32

time: 422 us -> 444 us (1.052)
  matrix products: 40.1 us -> 54.9 us
  waiting for transfers between devices: 170 us -> 163 us
  other arithmetic: 25 us -> 31.7 us
  local copies, waits for them, and re-layouts: 113 us -> 119 us
    all_gather x1 -> x0, waiting for transfers between devices: 71.6 us -> none  [body(): gathered = lax.all_gather(at_expert, 'req', axis=0, tiled=True)]
    ppermute x0 -> x3, waiting for transfers between devices: none -> 69 us  [the longest x2 69 us: gather_around(): lax.ppermute(going_up, axis, [(d, (d + 1) % ways) for d in range(ways)])]
    dynamic_update_slice x0 -> x4, local copies, waits for them, and re-layouts: none -> 13 us  [the longest x2 7.7 us: gather_around(): lax.dynamic_update_slice_in_dim(full, going_up, (here - far) % ways * ste...]
    all_gather x1 -> x0, local copies, waits for them, and re-layouts: 10.4 us -> none  [body(): gathered = lax.all_gather(at_expert, 'req', axis=0, tiled=True)]
    dot_general x4, matrix products: 3.33 us -> 13.4 us  [one_block(): jnp.einsum('gqts,sgd->gqtd', weights.astype(jnp.bfloat16), block_values,...]
    reduce_sum x4, other arithmetic: 2.83 us -> 9.06 us  [one_block(): running_sum = running_sum * factor + jnp.sum(weights, axis=-1)]
    dot_general x4, matrix products: 6.83 us -> 11.5 us  [one_block(): jnp.einsum('tgqd,sgd->gqts', query_fourfold, block_keys, preferred_elemen...]
    reduce_scatter x1, waiting for transfers between devices: 73.6 us -> 69.1 us  [body(): lax.psum_scatter(part_out, 'req', scatter_dimension=0, tiled=True)]
  transfers between devices with their start and end apart: 4 -> 6, of which waited for: 3 -> 4; matrix products, arithmetic and copies ran while one was open for 14% -> 16% of each run, Pallas kernels for 0% -> 0%
where the time goes in v1:
time: 444 us; the launch traced here: 441 us
  waiting for transfers between devices  163 us (37%)
  local copies, waits for them, and re-layouts  119 us (27%)
  matrix products  54.9 us (12%)
  blocking collectives  48.3 us (11%)
  other arithmetic  31.7 us (7%)
  between operations  13.6 us (3%)
  starting transfers between devices  10.7 us (2%)
    reduce_scatter x1, waiting for transfers between devices, body(): lax.psum_scatter(part_out, 'req', scatter_dimension=0, tiled=True)  69.1 us
    ppermute x2, waiting for transfers between devices, gather_around(): lax.ppermute(going_up, axis, [(d, (d + 1) % ways) for d in range(ways)])  69 us
    all_to_all x1, blocking collectives, body(): lax.all_to_all(outgoing, 'head', split_axis=0, concat_axis=0, tiled=True)  33.4 us
    all_gather x1, waiting for transfers between devices, body(): kv_piece = lax.all_gather(key_value_rows, 'head', axis=0, tiled=True)  25 us
    unnamed x34, local copies, waits for them, and re-layouts  16.6 us
    dot_general x1, local copies, waits for them, and re-layouts, body(): jnp.dot(normed, shared_gate_up.reshape(model_width, -1), preferred_elemen...  15.2 us
    all_to_all x1, blocking collectives, body(): lax.all_to_all(by_dest(packed), 'req', split_axis=0, concat_axis=0, tiled...  14.8 us
    dot_general x4, matrix products, one_block(): jnp.einsum('gqts,sgd->gqtd', weights.astype(jnp.bfloat16), block_values,...  13.4 us
  transfers between devices with their start and end apart: 6, of which 4 were waited for; matrix products, arithmetic and copies ran while one was open for 16% of the time, Pallas kernels for 0%

profile of v1, /device:TPU:1, one launch (start us, length us, event | category | flops | bytes accessed | tf_op | source)
XLA Modules:
  0.0 440.8 jit_solution(16055116626383563355)
XLA Ops:
  11.3 14.8 %all_to_all.15 = bf16[4,16,5120]{2,1,0:T(8,128)(2,1)S(1)} all-to-all(bf16[4,16,5120]{2,1,0:T(8,128)(2,1)S(1)} %broadcast_select_fusion), channel_id=1, replica_groups=mesh['req'=4,'head'=32] {'req'}, dimensions={0} | all-to-all | bytes 1310720 | tf_op jit(solution)/shard_map/all_to_all | solution.py:66
  50.1 25.0 %all-gather.2.cloned.1.call-done = bf16[2048,1024]{1,0:T(8,128)(2,1)} async-done(((bf16[64,1024]{1,0:T(8,128)(2,1)}), bf16[2048,1024]{1,0:T(8,128)(2,1)}) %all-gather.2.cloned.1.call-update) | async-done | bytes 4194320 | tf_op jit(solution)/shard_map/all_gather | solution.py:83
  75.0 61.0 %while.18 = (s32[]{:T(128)}, f32[4,4,64]{2,1,0:T(4,128)S(1)}, f32[4,4,64]{2,1,0:T(4,128)S(1)}, f32[4,4,64,128]{3,2,1,0:T(8,128)}, s32[64]{0:T(128)}, /*index=5*/...) while((s32[]{:T(128)}, f32[4,4,64]{2,1,0:T(4,128)S(1)}, ...), condition=%wide.region_4.5_spmd.clone, body=%wide.region_1.4_spmd.clone.sunk | while | flops 275748416 | bytes 13052895 | solution.py:121
  132.6 3.4 convolution_add_fusion.3
  144.5 3.6 reshape.171
  148.1 33.4 %all_to_all.16 = bf16[32,14,2048]{2,1,0:T(8,128)(2,1)S(1)} all-to-all(bf16[32,14,2048]{2,1,0:T(8,128)(2,1)} %reshape.171), channel_id=1, replica_groups=mesh['req'=4,'head'=32] {'head'}, dimensions={0} | all-to-all | bytes 3670016 | tf_op jit(solution)/shard_map/all_to_all | solution.py:147
  187.9 40.3 %collective-permute-done = bf16[32,14,2048]{2,0,1:T(8,128)(2,1)} collective-permute-done((bf16[32,14,2048]{2,0,1:T(8,128)(2,1)}, bf16[32,14,2048]{2,0,1:T(8,128)(2,1)}, u32[]{:S(2)}, u32[]{:S(2)}) %collective-permute-start) | collective-permute-done | bytes 1835040 | tf_op jit(solution)/shard_map/ppermute | solution.py:23
  228.2 4.3 broadcast_in_dim.89
  234.0 3.9 copy_dynamic-update-slice_fusion.2
  237.8 3.8 copy_dynamic-update-slice_fusion.1
  241.6 28.7 %collective-permute-done.2 = bf16[32,14,2048]{2,0,1:T(8,128)(2,1)} collective-permute-done((bf16[32,14,2048]{2,0,1:T(8,128)(2,1)}, bf16[32,14,2048]{2,0,1:T(8,128)(2,1)}, u32[]{:S(2)}, u32[]{:S(2)}) %collective-permute-start.2) | collective-permute-done | bytes 1835040 | tf_op jit(solution)/shard_map/ppermute | solution.py:23
  270.3 3.8 copy_dynamic-update-slice_fusion
  274.2 10.5 %reshape.196 = bf16[1792,2048,1]{1,0,2:T(8,128)(2,1)} reshape(bf16[128,14,2048]{2,1,0:T(8,128)(2,1)} %copy_dynamic-update-slice_fusion) | data formatting | bytes 14680064 | tf_op jit(solution)/shard_map/reshape | solution.py:149
  284.7 8.6 %fusion.14 = f32[1792,2,352]{0,2,1:T(8,128)S(1)} fusion(bf16[1792,2048,1]{1,0,2:T(8,128)(2,1)} %reshape.196, bf16[1,2,352,2048]{3,2,1,0:T(8,128)(2,1)S(1)} %copy-done), kind=kOutput, calls=%fused_computation.28 | convolution fusion | flops 5167382528 | bytes 15269888 | tf_op jit(solution)/shard_map/nd,kfd->nkf/dot_general | solution.py:150
  293.3 6.2 %convolution_convert_fusion = bf16[1792,2048]{1,0:T(8,128)(2,1)} fusion(bf16[1,352,2048]{2,1,0:T(8,128)(2,1)S(1)} %copy-done.14, f32[1792,2,352]{0,2,1:T(8,128)S(1)} %fusion.14), kind=kOutput, calls=%fused_computation.25 | convolution fusion | flops 2590515200 | bytes 13828096 | tf_op jit(solution)/shard_map/dot_general | solution.py:154
  299.5 69.1 %reduce-scatter.2.cloned.1.call-done = bf16[448,2048]{1,0:T(8,128)(2,1)} async-done(((bf16[1792,2048]{1,0:T(8,128)(2,1)}), bf16[448,2048]{1,0:T(8,128)(2,1)}) %reduce-scatter.2.cloned.1.call-update) | async-done | bytes 1835024 | tf_op jit(solution)/shard_map/reduce_scatter | solution.py:157
  368.6 3.6 reshape.173
  372.3 7.9 %all-to-all-start.2 = ((bf16[32,14,2048]{2,1,0:T(8,128)(2,1)}), bf16[32,14,2048]{2,1,0:T(8,128)(2,1)}, u32[]{:S(2)}, u32[]{:S(2)}) async-start(bf16[32,14,2048]{2,1,0:T(8,128)(2,1)} %reshape.173), calls=%async_computation.3 | async-start | bytes 4194304 | tf_op jit(solution)/shard_map/all_to_all | solution.py:158
  380.7 11.3 %copy.91 = bf16[256,8,2,1408]{3,1,2,0:T(8,128)(2,1)} copy(bf16[256,8,2,1408]{3,2,1,0:T(2,128)(2,1)} %bitcast.103) | data formatting | bytes 23068672
  391.9 15.2 %copy.68 = bf16[2816,2048]{1,0:T(8,128)(2,1)} copy(bf16[2816,2048]{0,1:T(8,128)(2,1)} %bitcast.101) | data formatting | bytes 23068672 | tf_op jit(solution)/shard_map/dot_general | solution.py:142
  407.2 8.7 %fusion.25 = f32[64,2,1408]{2,0,1:T(8,128)} fusion(bf16[2,1408,2048]{2,1,0:T(8,128)(2,1)} %bitcast.100, bf16[64,2048]{1,0:T(8,128)(2,1)S(1)} %copy-done.7), kind=kOutput, calls=%fused_computation.52 | convolution fusion | flops 738197504 | bytes 12517376 | tf_op jit(solution)/shard_map/dot_general | solution.py:142
  421.6 3.7 gather.12
  425.3 4.2 multiply_reduce_fusion
  429.5 4.5 %fusion.18 = bf16[64,2048]{1,0:T(8,128)(2,1)} fusion(f32[64,2048]{1,0:T(8,128)S(1)} %multiply_reduce_fusion, bf16[1408,2048]{1,0:T(8,128)(2,1)} %param.23, f32[64,2,1408]{2,0,1:T(8,128)S(1)} %copy-done.5, f32[64,2048]{1,0:T(8,128)S(1)} %reshape.167, bf16[64,5120]{1,0:T(8,128)(2,1)} %bitcast.108), kind=kOutput, calls=%fused_computation.34 | convolution fusion | flops 370204672 | bytes 8060928 | tf_op jit(solution)/shard_map/dot_general | solution.py:146
  (135 shorter events, 108.5 us)
Async XLA Ops:
  6.5 278.2 %copy-start = (bf16[1,2,352,2048]{3,2,1,0:T(8,128)(2,1)S(1)}, bf16[1,2,352,2048]{3,2,1,0:T(8,128)(2,1)}, u32[]{:S(2)}) copy-start(bf16[1,2,352,2048]{3,2,1,0:T(8,128)(2,1)} %param.24) | copy-start | bytes 8650756
  6.5 68.5 %all-gather.2.cloned.1.call-start = ((), (), s32[]{:S(2)}) async-start(), calls=%async_computation.4 | async-start | bytes 4325376 | tf_op jit(solution)/shard_map/all_gather | solution.py:83
  26.1 48.9 %copy-start.4 = (bf16[4,16,5120]{2,1,0:T(8,128)(2,1)}, bf16[4,16,5120]{2,1,0:T(8,128)(2,1)S(1)}, u32[]{:S(2)}) copy-start(bf16[4,16,5120]{2,1,0:T(8,128)(2,1)S(1)} %all_to_all.15) | copy-start | bytes 1966084
  26.8 341.8 %reduce-scatter.2.cloned.1.call-start = ((), (), s32[]{:S(2)}) async-start(), calls=%async_computation.5 | async-start | bytes 9175040 | tf_op jit(solution)/shard_map/reduce_scatter | solution.py:157
  136.0 4.8 %copy-start.11 = (f32[2048]{0:T(1024)S(1)}, f32[2048]{0:T(1024)}, u32[]{:S(2)}) copy-start(f32[2048]{0:T(1024)} %param.21) | copy-start | bytes 24580
  137.3 5.3 %copy-start.8 = (pred[448,64]{0,1:T(8,128)(4,1)S(1)}, pred[448,64]{0,1:T(8,128)(4,1)}, u32[]{:S(2)}) copy-start(pred[448,64]{0,1:T(8,128)(4,1)} %fusion.22) | copy-start | bytes 86020
  141.9 0.7 copy-start.6
  181.6 1.4 copy-start.2
  185.2 43.0 %collective-permute-start = (bf16[32,14,2048]{2,0,1:T(8,128)(2,1)}, bf16[32,14,2048]{2,0,1:T(8,128)(2,1)}, u32[]{:S(2)}, u32[]{:S(2)}) collective-permute-start(bf16[32,14,2048]{2,0,1:T(8,128)(2,1)} %copy.74), channel_id=1, source_target_pairs={{0,32},{32,64},{64,96},{96,0},{1,33},{33,65},{65,97},{97,1},{2,34}... | collective-permute-start | bytes 5505032 | tf_op jit(solution)/shard_map/ppermute | solution.py:23
  186.4 51.4 %collective-permute-start.1 = (bf16[32,14,2048]{2,0,1:T(8,128)(2,1)}, bf16[32,14,2048]{2,0,1:T(8,128)(2,1)}, u32[]{:S(2)}, u32[]{:S(2)}) collective-permute-start(bf16[32,14,2048]{2,0,1:T(8,128)(2,1)} %copy.74), channel_id=1, source_target_pairs={{0,96},{32,0},{64,32},{96,64},{1,97},{33,1},{65,33},{97,65},{2,98}... | collective-permute-start | bytes 5505032 | tf_op jit(solution)/shard_map/ppermute | solution.py:26
  228.2 42.1 %collective-permute-start.2 = (bf16[32,14,2048]{2,0,1:T(8,128)(2,1)}, bf16[32,14,2048]{2,0,1:T(8,128)(2,1)}, u32[]{:S(2)}, u32[]{:S(2)}) collective-permute-start(bf16[32,14,2048]{2,0,1:T(8,128)(2,1)} %collective-permute-done), channel_id=1, source_target_pairs={{0,32},{32,64},{64,96},{96,0},{1,33},{33,65},{65,97},{97,1},{2,34}... | collective-permute-start | bytes 5505032 | tf_op jit(solution)/shard_map/ppermute | solution.py:23
  228.2 4.3 copy-start.3
  284.7 8.6 %copy-start.14 = (bf16[1,352,2048]{2,1,0:T(8,128)(2,1)S(1)}, bf16[1,352,2048]{2,1,0:T(8,128)(2,1)}, u32[]{:S(2)}) copy-start(bf16[1,352,2048]{2,1,0:T(8,128)(2,1)} %param.25) | copy-start | bytes 4325380
  372.2 8.0 %copy-start.9 = (s32[64,6]{0,1:T(8,128)S(1)}, s32[64,6]{0,1:T(8,128)}, u32[]{:S(2)}) copy-start(s32[64,6]{0,1:T(8,128)} %param.19) | copy-start | bytes 4612
  372.3 8.2 %copy-start.13 = (pred[64,6]{0,1:T(8,128)(4,1)S(1)}, pred[64,6]{0,1:T(8,128)(4,1)}, u32[]{:S(2)}) copy-start(pred[64,6]{0,1:T(8,128)(4,1)} %get-tuple-element.260) | copy-start | bytes 1156
  372.3 8.3 %copy-start.12 = (f32[64,6]{0,1:T(8,128)S(1)}, f32[64,6]{0,1:T(8,128)}, u32[]{:S(2)}) copy-start(f32[64,6]{0,1:T(8,128)} %param.20) | copy-start | bytes 4612
  372.3 43.7 %all-to-all-start.2 = ((bf16[32,14,2048]{2,1,0:T(8,128)(2,1)}), bf16[32,14,2048]{2,1,0:T(8,128)(2,1)}, u32[]{:S(2)}, u32[]{:S(2)}) async-start(bf16[32,14,2048]{2,1,0:T(8,128)(2,1)} %reshape.173), calls=%async_computation.3 | async-start | bytes 4194304 | tf_op jit(solution)/shard_map/all_to_all | solution.py:158
  391.9 15.2 %copy-start.10 = (s32[384]{0:T(512)S(1)}, s32[384]{0:T(512)}, u32[]{:S(2)}) copy-start(s32[384]{0:T(512)} %fusion.30) | copy-start | bytes 4612
  391.9 15.2 %copy-start.7 = (bf16[64,2048]{1,0:T(8,128)(2,1)S(1)}, bf16[64,2048]{1,0:T(8,128)(2,1)}, u32[]{:S(2)}) copy-start(bf16[64,2048]{1,0:T(8,128)(2,1)} %copy-done.6) | copy-start | bytes 786436
  425.3 4.2 copy-start.5
  425.3 8.7 %copy-start.1 = (bf16[1,2,352,2048]{3,2,1,0:T(8,128)(2,1)S(1)}, bf16[1,2,352,2048]{3,2,1,0:T(8,128)(2,1)}, u32[]{:S(2)}) copy-start(bf16[1,2,352,2048]{3,2,1,0:T(8,128)(2,1)} %param.24) | copy-start | bytes 8650756
Sparse Core Ops, SparseCore 0:
  26.9 48.0 all-gather.1
  299.6 68.9 reduce-scatter.1
